TPU v7x, 32 devices: a whole 2x2x4 slice. The times are simulated.
32 devices in a mesh: rows: 8 (over z, y), cols: 4 (over x, core).
Axes of the slice: x: 2, y: 2, z: 4, core: 2. Of those that a mesh axis runs over, the one named last changes fastest.
Arguments:
- snapshots: float32 [512, 65536], P(('cols', 'rows'))
- pair_table: int32 [4], replicated, may hold values from 0 to 3, as said below
Outputs:
- rotated: float32 [512, 65536], P('cols', 'rows')
Inputs may be any that keep to these rules, and one draw needn't show every extreme that they name: pair_table[c] = c XOR m for one m shared by all c, m a power of two below 4, so blocks are paired two by two along one binary digit.
All inputs are finite; a program needn't handle non-finite values.
Results may differ from a plain program's by a relative error of at most 0.0003.
Values sent between devices are 32-bit elements; how exact they have to be, the bound alone decides.
No kernel may reach another device: no remote copies, remote signals or barrier semaphores. Data moves between devices by JAX's collectives and lax.ppermute only.
A program may use at most 64 MiB of HBM per device.

v0:
```python
import functools

import jax
import jax.numpy as jnp
import numpy as np
from jax import lax
from jax.experimental import pallas as pl
from jax.experimental.pallas import tpu as pltpu
from jax.sharding import PartitionSpec as P

ROUNDS = 8


def partner_2(value, axis, bit):
    mask = 2**bit
    pairs = [(source, source ^ mask) for source in range(lax.axis_size(axis))]
    return lax.ppermute(value, axis, pairs)


def jacobi_kernel(gram_ref, rotation_ref):
    highest = lax.Precision.HIGHEST
    order_dim = gram_ref.shape[0]
    last_idx = order_dim - 1
    width = order_dim // 2
    gram = gram_ref[...]
    row_col = lax.broadcasted_iota(jnp.int32, (order_dim, 1), 0)
    row_full = lax.broadcasted_iota(jnp.int32, (order_dim, order_dim), 0)
    col_full = lax.broadcasted_iota(jnp.int32, (order_dim, order_dim), 1)
    eye = row_full == col_full
    rotation = None
    for round_idx in range(ROUNDS):
        fixed = round_idx % last_idx
        mirror = 2 * fixed - row_col
        mirror = jnp.where(mirror < 0, mirror + last_idx, mirror)
        partner = jnp.where(row_col == fixed, last_idx, jnp.where(row_col == last_idx, fixed, mirror))
        offset = row_col - fixed
        offset = jnp.where(offset < 0, offset + last_idx, offset)
        is_first = (row_col == last_idx) | ((row_col != fixed) & (offset >= 1) & (offset <= width - 1))
        swap = (col_full == partner).astype(jnp.float32)
        on_diag = jnp.where(eye, gram, 0.0)
        diag_own = jnp.sum(on_diag, axis=1, keepdims=True)
        diag_row = jnp.sum(on_diag, axis=0, keepdims=True)
        diag_mate = jnp.sum(swap * diag_row, axis=1, keepdims=True)
        picked = gram * swap
        cross_second = jnp.sum(picked, axis=1, keepdims=True)
        cross_row = jnp.sum(picked, axis=0, keepdims=True)
        cross_first = jnp.sum(jnp.where(eye, cross_row, 0.0), axis=1, keepdims=True)
        cross_val = jnp.where(is_first, cross_first, cross_second)
        spread = jnp.where(is_first, diag_mate - diag_own, diag_own - diag_mate)
        hypot_val = jnp.sqrt(spread * spread + 4.0 * cross_val * cross_val)
        denom = jnp.sqrt(2.0 * hypot_val * (hypot_val + jnp.abs(spread)))
        sign_val = jnp.where(spread >= 0.0, 1.0, -1.0)
        cosine = (hypot_val + jnp.abs(spread)) / denom
        sine_val = 2.0 * cross_val * sign_val / denom
        signed = jnp.where(is_first, sine_val, -sine_val)
        diag_part = jnp.where(eye, cosine, 0.0)
        turn = diag_part + swap * signed
        turn_t = diag_part - swap * signed
        gram = jnp.dot(
            turn_t,
            jnp.dot(gram, turn, precision=highest, preferred_element_type=jnp.float32),
            precision=highest,
            preferred_element_type=jnp.float32,
        )
        rotation = turn if rotation is None else jnp.dot(
            rotation, turn, precision=highest, preferred_element_type=jnp.float32
        )
    rotation_ref[...] = rotation

def jacobi_pallas(gram):
    return pl.pallas_call(
        jacobi_kernel,
        out_shape=jax.ShapeDtypeStruct(gram.shape, jnp.float32),
        in_specs=[pl.BlockSpec(memory_space=pltpu.VMEM)],
        out_specs=pl.BlockSpec(memory_space=pltpu.VMEM),
    )(gram)


def gram_kernel(mine_ref, theirs_ref, out_ref, acc_ref):
    step = pl.program_id(0)

    @pl.when(step == 0)
    def _():
        acc_ref[...] = jnp.zeros_like(acc_ref)

    stacked = jnp.concatenate([mine_ref[...], theirs_ref[...]], 0)
    acc_ref[...] += lax.dot_general(
        stacked,
        stacked,
        (((1,), (1,)), ((), ())),
        precision=lax.Precision.HIGHEST,
        preferred_element_type=jnp.float32,
    )

    @pl.when(step == pl.num_programs(0) - 1)
    def _():
        width = mine_ref.shape[0]
        out_ref[0] = acc_ref[:width, :width]
        out_ref[1] = acc_ref[:width, width:]
        out_ref[2] = acc_ref[width:, width:]


def pair_terms(mine, theirs):
    width, cells = mine.shape
    tile = min(cells, 2048)
    cell_spec = pl.BlockSpec((width, tile), lambda step: (0, step))
    return pl.pallas_call(
        gram_kernel,
        out_shape=jax.ShapeDtypeStruct((3, width, width), jnp.float32),
        grid=(cells // tile,),
        in_specs=[cell_spec, cell_spec],
        out_specs=pl.BlockSpec((3, width, width), lambda step: (0, 0, 0)),
        scratch_shapes=[pltpu.VMEM((2 * width, 2 * width), jnp.float32)],
        cost_estimate=pl.CostEstimate(
            flops=8 * width * width * cells, transcendentals=0, bytes_accessed=8 * width * cells
        ),
    )(mine, theirs)


def row_total(part):
    count = lax.axis_size("rows")
    bit = 1
    while bit < count:
        pairs = [(source, source ^ bit) for source in range(count)]
        part = part + lax.ppermute(part, "rows", pairs)
        bit *= 2
    return part


CHUNKS = 4


def lay_kernel(source_ref, *out_refs):
    piece = out_refs[0].shape[-1]
    for chunk, out_ref in enumerate(out_refs):
        out_ref[...] = source_ref[:, chunk * piece : (chunk + 1) * piece]


def lay_out(snapshots, rows_n, chunks):
    local_rows, cells = snapshots.shape
    width = cells // rows_n
    piece = width // chunks
    out_spec = pl.BlockSpec((None, local_rows, piece), lambda dest: (dest, 0, 0))
    return pl.pallas_call(
        lay_kernel,
        out_shape=[jax.ShapeDtypeStruct((rows_n, local_rows, piece), snapshots.dtype)] * chunks,
        grid=(rows_n,),
        in_specs=[pl.BlockSpec((local_rows, width), lambda dest: (0, dest))],
        out_specs=[out_spec] * chunks,
        cost_estimate=pl.CostEstimate(flops=0, transcendentals=0, bytes_accessed=8 * local_rows * cells),
    )(snapshots)


def exchange(bit_pos, snapshots):
    chunks = 1 if bit_pos == 0 else CHUNKS
    rows_n = lax.axis_size("rows")
    local_rows, cells = snapshots.shape
    width = cells // rows_n
    piece = width // chunks

    sends = lay_out(snapshots, rows_n, chunks)

    def laid(chunk):
        return sends[chunk]

    def spread(sent):
        got = lax.all_to_all(sent, "rows", split_axis=0, concat_axis=0)
        return got.reshape(rows_n * local_rows, piece)

    own_parts = [spread(laid(0))]
    other_parts = []
    for chunk in range(1, chunks):
        held = (own_parts[-1], laid(chunk)) + tuple(other_parts[-1:])
        held = lax.optimization_barrier(held)
        own_parts[-1] = held[0]
        if other_parts:
            other_parts[-1] = held[2]
        other_parts.append(partner_2(held[0], "cols", bit_pos))
        own_parts.append(spread(held[1]))
    other_parts.append(partner_2(own_parts[-1], "cols", bit_pos))
    terms = None
    for mine, theirs in zip(own_parts, other_parts):
        part = pair_terms(mine, theirs)
        terms = part if terms is None else terms + part
    return jnp.concatenate(own_parts, 1), jnp.concatenate(other_parts, 1), terms


def assemble(terms, own_low):
    gram_mine, gram_mixed, gram_theirs = terms[0], terms[1], terms[2]
    upper_left = jnp.where(own_low, gram_mine, gram_theirs)
    lower_right = jnp.where(own_low, gram_theirs, gram_mine)
    upper_right = jnp.where(own_low, gram_mixed, gram_mixed.T)
    top_rows = jnp.concatenate([upper_left, upper_right], 1)
    bottom_rows = jnp.concatenate([upper_right.T, lower_right], 1)
    return jnp.concatenate([top_rows, bottom_rows], 0)


def rotate_kernel(coef_ref, mine_ref, theirs_ref, out_ref):
    stacked = jnp.concatenate([mine_ref[...], theirs_ref[...]], 0)
    out_ref[...] = jnp.dot(
        coef_ref[...], stacked, precision=lax.Precision.HIGHEST, preferred_element_type=jnp.float32
    )


def rotate_part(columns_sel, own_low, mine, theirs):
    width, cells = mine.shape
    coef_mine = jnp.where(own_low, columns_sel[:width], columns_sel[width:])
    coef_theirs = jnp.where(own_low, columns_sel[width:], columns_sel[:width])
    coef = jnp.concatenate([coef_mine, coef_theirs], 0).T
    tile = min(cells, 2048)
    coef_spec = pl.BlockSpec((width, 2 * width), lambda step: (0, 0))
    cell_spec = pl.BlockSpec((width, tile), lambda step: (0, step))
    return pl.pallas_call(
        rotate_kernel,
        out_shape=jax.ShapeDtypeStruct((width, cells), jnp.float32),
        grid=(cells // tile,),
        in_specs=[coef_spec, cell_spec, cell_spec],
        out_specs=cell_spec,
        cost_estimate=pl.CostEstimate(
            flops=4 * width * width * cells, transcendentals=0, bytes_accessed=12 * width * cells
        ),
    )(coef, mine, theirs)


def shards(snapshots, pair_table):
    bit_count = lax.axis_size("cols").bit_length() - 1
    column = lax.axis_index("cols")
    mask_val = pair_table[0]
    bit_index = jnp.int32(0)
    for bit_pos in range(bit_count):
        bit_index = bit_index + (mask_val >> bit_pos & 1) * bit_pos
    partner = jnp.bitwise_xor(column, mask_val)
    own_low = column < partner
    branches = [functools.partial(exchange, bit_pos) for bit_pos in range(bit_count)]
    own_parts, other_parts, terms = lax.switch(bit_index, branches, snapshots)
    gram_full = assemble(row_total(terms), own_low)
    rotation = jacobi_pallas(gram_full)
    width = own_parts.shape[0]
    own_columns = jnp.where(own_low, rotation[:, :width], rotation[:, width:])
    return rotate_part(own_columns, own_low, own_parts, other_parts)


def solution(mesh):
    in_specs = (P(("cols", "rows"), None), P())
    out_specs = P("cols", "rows")
    return jax.shard_map(shards, mesh=mesh, in_specs=in_specs, out_specs=out_specs, check_vma=False)
```

profile of v0, /device:TPU:0, one launch (start us, length us, event | category | flops | bytes accessed | tf_op | source)
XLA Modules:
  0.0 172.4 jit_solution(2169168864600437814)
XLA Ops:
  0.7 0.0 copy-start.8
  0.7 125.6 %conditional.1 = (f32[128,8192]{1,0:T(8,128)}, f32[128,8192]{1,0:T(8,128)}, f32[3,128,128]{2,1,0:T(8,128)S(1)}) conditional(s32[]{:T(128)} %clamp.3, f32[16,65536]{1,0:T(8,128)} %param.4, f32[16,65536]{1,0:T(8,128)} %param.4), branch_computations={%region_0.0_spmd, %region_1.0_spmd} | conditional | flops 1080180736 | bytes 81986016 | solution.py:235
  0.7 6.6 %branch_0_fun.2 = f32[8,16,8192]{2,1,0:T(8,128)} custom-call(f32[16,65536]{1,0:T(8,128)} %source_ref), custom_call_target="tpu_custom_call" | custom-call | bytes 8388608 | tf_op jit(solution)/shard_map/cond/branch_0_fun/pallas_call | solution.py:144
  7.3 100.5 %all_to_all.20 = f32[8,16,8192]{2,1,0:T(8,128)S(1)} all-to-all(f32[8,16,8192]{2,1,0:T(8,128)} %branch_0_fun.2), channel_id=1, replica_groups=mesh['rows'=8,'cols'=4] {'rows'}, dimensions={0} | all-to-all | bytes 8388608 | tf_op jit(solution)/shard_map/cond/branch_0_fun/all_to_all | solution.py:167
  107.7 1.9 %copy-done = f32[8,16,8192]{2,1,0:T(8,128)} copy-done((f32[8,16,8192]{2,1,0:T(8,128)}, f32[8,16,8192]{2,1,0:T(8,128)S(1)}, u32[]{:S(2)}) %copy-start) | copy-done | bytes 4194328 | tf_op jit(solution)/shard_map/cond
  109.7 0.0 collective-permute-start
  109.7 7.3 %collective-permute-done.theirs_ref = f32[128,8192]{1,0:T(8,128)} collective-permute-done((f32[128,8192]{1,0:T(8,128)S(1)}, f32[128,8192]{1,0:T(8,128)}, u32[]{:S(2)}, u32[]{:S(2)}) %collective-permute-start) | collective-permute-done | bytes 4194336 | tf_op jit(solution)/shard_map/cond/branch_0_fun/ppermute | solution.py:17
  117.0 9.1 %branch_0_fun.3 = f32[3,128,128]{2,1,0:T(8,128)S(1)} custom-call(f32[128,8192]{1,0:T(8,128)} %bitcast.20, f32[128,8192]{1,0:T(8,128)} %collective-permute-done.theirs_ref), custom_call_target="tpu_custom_call" | custom-call | flops 1073741824 | bytes 8388608 | tf_op jit(solution)/shard_map/cond/branch_0_fun/pallas_call | solution.py:107
  126.3 1.5 collective-permute-start.5
  127.8 5.5 %collective-permute-done.5 = f32[3,128,128]{2,1,0:T(8,128)S(1)} collective-permute-done((f32[3,128,128]{2,1,0:T(8,128)S(1)}, f32[3,128,128]{2,1,0:T(8,128)S(1)}, u32[]{:S(2)}, u32[]{:S(2)}) %collective-permute-start.5) | collective-permute-done | bytes 196640 | tf_op jit(solution)/shard_map/ppermute | solution.py:125
  133.3 1.2 collective-permute-start.6
  134.5 5.0 %collective-permute-done.6 = f32[3,128,128]{2,1,0:T(8,128)S(1)} collective-permute-done((f32[3,128,128]{2,1,0:T(8,128)S(1)}, f32[3,128,128]{2,1,0:T(8,128)S(1)}, u32[]{:S(2)}, u32[]{:S(2)}) %collective-permute-start.6) | collective-permute-done | bytes 196640 | tf_op jit(solution)/shard_map/ppermute | solution.py:125
  139.5 1.1 collective-permute-start.7
  140.6 0.0 copy-done.8
  140.7 9.2 %collective-permute-done.7 = f32[3,128,128]{2,1,0:T(8,128)S(1)} collective-permute-done((f32[3,128,128]{2,1,0:T(8,128)S(1)}, f32[3,128,128]{2,1,0:T(8,128)S(1)}, u32[]{:S(2)}, u32[]{:S(2)}) %collective-permute-start.7) | collective-permute-done | bytes 196640 | tf_op jit(solution)/shard_map/ppermute | solution.py:125
  149.9 0.1 copy.3
  150.0 0.1 copy.4
  150.1 0.7 maximum_maximum_fusion.gram_ref
  150.9 11.8 %shard_map.34 = f32[256,256]{1,0:T(8,128)} custom-call(f32[256,256]{1,0:T(8,128)} %maximum_maximum_fusion.gram_ref), custom_call_target="tpu_custom_call" | custom-call | tf_op jit(solution)/shard_map/pallas_call | solution.py:71
  162.6 1.0 fusion
  163.6 0.1 copy.7
  163.7 0.1 copy.8
  163.9 0.7 maximum_bitcast_fusion.coef_ref
  164.5 7.9 %shard_map.35 = f32[128,8192]{1,0:T(8,128)} custom-call(f32[128,256]{1,0:T(8,128)} %maximum_bitcast_fusion.coef_ref, f32[128,8192]{1,0:T(8,128)} %get-tuple-element.23.mine_ref, f32[128,8192]{1,0:T(8,128)} %get-tuple-element.24.theirs_ref), custom_call_target="tpu_custom_call" | custom-call | flops 536870912 | bytes 12582912 | tf_op jit(solution)/shard_map/pallas_call | solution.py:213
  (8 shorter events, 0.1 us)
Async XLA Ops:
  0.7 140.0 %copy-start.8 = (s32[4]{0:T(128)S(1)}, s32[4]{0:T(128)}, u32[]{:S(2)}) copy-start(s32[4]{0:T(128)} %param.5) | copy-start | bytes 52
  107.7 2.0 %copy-start = (f32[8,16,8192]{2,1,0:T(8,128)}, f32[8,16,8192]{2,1,0:T(8,128)S(1)}, u32[]{:S(2)}) copy-start(f32[8,16,8192]{2,1,0:T(8,128)S(1)} %all_to_all.20) | copy-start | bytes 12582916 | tf_op jit(solution)/shard_map/cond
  109.7 7.3 %collective-permute-start = (f32[128,8192]{1,0:T(8,128)S(1)}, f32[128,8192]{1,0:T(8,128)}, u32[]{:S(2)}, u32[]{:S(2)}) collective-permute-start(f32[128,8192]{1,0:T(8,128)S(1)} %bitcast.19), channel_id=1, source_target_pairs={{0,1},{1,0},{2,3},{3,2},{4,5},{5,4},{6,7},{7,6},{8,9},{9,8},{10,11... | collective-permute-start | bytes 12582920 | tf_op jit(solution)/shard_map/cond/branch_0_fun/ppermute | solution.py:17
  126.3 7.0 %collective-permute-start.5 = (f32[3,128,128]{2,1,0:T(8,128)S(1)}, f32[3,128,128]{2,1,0:T(8,128)S(1)}, u32[]{:S(2)}, u32[]{:S(2)}) collective-permute-start(f32[3,128,128]{2,1,0:T(8,128)S(1)} %get-tuple-element.22), channel_id=1, source_target_pairs={{0,4},{4,0},{8,12},{12,8},{16,20},{20,16},{24,28},{28,24},{1,5},{5... | collective-permute-start | bytes 589832 | tf_op jit(solution)/shard_map/ppermute | solution.py:125
  133.3 6.2 %collective-permute-start.6 = (f32[3,128,128]{2,1,0:T(8,128)S(1)}, f32[3,128,128]{2,1,0:T(8,128)S(1)}, u32[]{:S(2)}, u32[]{:S(2)}) collective-permute-start(f32[3,128,128]{2,1,0:T(8,128)S(1)} %add.18), channel_id=1, source_target_pairs={{0,8},{4,12},{8,0},{12,4},{16,24},{20,28},{24,16},{28,20},{1,9},{5... | collective-permute-start | bytes 589832 | tf_op jit(solution)/shard_map/ppermute | solution.py:125
  139.5 10.4 %collective-permute-start.7 = (f32[3,128,128]{2,1,0:T(8,128)S(1)}, f32[3,128,128]{2,1,0:T(8,128)S(1)}, u32[]{:S(2)}, u32[]{:S(2)}) collective-permute-start(f32[3,128,128]{2,1,0:T(8,128)S(1)} %add.19), channel_id=1, source_target_pairs={{0,16},{4,20},{8,24},{12,28},{16,0},{20,4},{24,8},{28,12},{1,17},{... | collective-permute-start | bytes 589832 | tf_op jit(solution)/shard_map/ppermute | solution.py:125
where the time goes:
time: 173 us; the launch traced here: 172 us
  blocking collectives  100 us (58%)
  Pallas kernels  35.4 us (20%)
  waiting for transfers between devices  27 us (16%)
  starting transfers between devices  3.83 us (2%)
  local copies, waits for them, and re-layouts  3.3 us (2%)
    all_to_all x1, blocking collectives, spread(): got = lax.all_to_all(sent, 'rows', split_axis=0, concat_axis=0)  100 us
    ppermute x3, waiting for transfers between devices, row_total(): part = part + lax.ppermute(part, 'rows', pairs)  19.7 us
    pallas_call x1, Pallas kernels, jacobi_pallas(): pl.pallas_call(jacobi_kernel, out_shape=jax.ShapeDtypeStruct(gram.shape,...  11.8 us
    pallas_call x1, Pallas kernels, pair_terms(): pl.pallas_call(gram_kernel, out_shape=jax.ShapeDtypeStruct((3, width, wid...  9.1 us
    pallas_call x1, Pallas kernels, rotate_part(): pl.pallas_call(rotate_kernel, out_shape=jax.ShapeDtypeStruct((width, cell...  7.9 us
    ppermute x1, waiting for transfers between devices, partner_2(): return lax.ppermute(value, axis, pairs)  7.29 us
    pallas_call x1, Pallas kernels, lay_out(): pl.pallas_call(lay_kernel, out_shape=[jax.ShapeDtypeStruct((rows_n, local...  6.59 us
    ppermute x3, starting transfers between devices, row_total(): part = part + lax.ppermute(part, 'rows', pairs)  3.83 us
  transfers between devices with their start and end apart: 4, of which 4 were waited for; matrix products, arithmetic and copies ran while one was open for 0% of the time, Pallas kernels for 0%

commit v1 on v0

--- a/solution.py
+++ b/solution.py
@@ -100,6 +100,35 @@
         out_ref[2] = acc_ref[width:, width:]
 
 
+def gram_store_kernel(mine_ref, theirs_ref, own_in, other_in, out_ref, own_ref, other_ref, acc_ref):
+    del own_in, other_in
+    gram_kernel(mine_ref, theirs_ref, out_ref, acc_ref)
+    own_ref[...] = mine_ref[...]
+    other_ref[...] = theirs_ref[...]
+
+
+def pair_terms_stored(mine, theirs, own_full, other_full, chunk):
+    width, piece = mine.shape
+    cell_spec = pl.BlockSpec((width, piece), lambda step: (0, 0))
+    full_spec = pl.BlockSpec((width, piece), lambda step: (0, chunk))
+    return pl.pallas_call(
+        gram_store_kernel,
+        out_shape=[
+            jax.ShapeDtypeStruct((3, width, width), jnp.float32),
+            jax.ShapeDtypeStruct(own_full.shape, own_full.dtype),
+            jax.ShapeDtypeStruct(other_full.shape, other_full.dtype),
+        ],
+        grid=(1,),
+        in_specs=[cell_spec, cell_spec, pl.BlockSpec(memory_space=pl.ANY), pl.BlockSpec(memory_space=pl.ANY)],
+        out_specs=[pl.BlockSpec((3, width, width), lambda step: (0, 0, 0)), full_spec, full_spec],
+        scratch_shapes=[pltpu.VMEM((2 * width, 2 * width), jnp.float32)],
+        input_output_aliases={2: 1, 3: 2},
+        cost_estimate=pl.CostEstimate(
+            flops=8 * width * width * piece, transcendentals=0, bytes_accessed=16 * width * piece
+        ),
+    )(mine, theirs, own_full, other_full)
+
+
 def pair_terms(mine, theirs):
     width, cells = mine.shape
     tile = min(cells, 2048)
@@ -178,11 +207,15 @@
         other_parts.append(partner_2(held[0], "cols", bit_pos))
         own_parts.append(spread(held[1]))
     other_parts.append(partner_2(own_parts[-1], "cols", bit_pos))
+    if chunks == 1:
+        return own_parts[0], other_parts[0], pair_terms(own_parts[0], other_parts[0])
+    own_full = jnp.zeros((rows_n * local_rows, width), snapshots.dtype)
+    other_full = jnp.zeros((rows_n * local_rows, width), snapshots.dtype)
     terms = None
-    for mine, theirs in zip(own_parts, other_parts):
-        part = pair_terms(mine, theirs)
+    for chunk, (mine, theirs) in enumerate(zip(own_parts, other_parts)):
+        part, own_full, other_full = pair_terms_stored(mine, theirs, own_full, other_full, chunk)
         terms = part if terms is None else terms + part
-    return jnp.concatenate(own_parts, 1), jnp.concatenate(other_parts, 1), terms
+    return own_full, other_full, terms
 
 
 def assemble(terms, own_low):

time: 173 us -> 173 us (level)
  no operation moved by 1% of the time
where the time goes in v1:
time: 173 us; the launch traced here: 172 us
  blocking collectives  100 us (58%)
  Pallas kernels  35.4 us (20%)
  waiting for transfers between devices  27 us (16%)
  starting transfers between devices  3.83 us (2%)
  local copies, waits for them, and re-layouts  3.31 us (2%)
    all_to_all x1, blocking collectives, spread(): got = lax.all_to_all(sent, 'rows', split_axis=0, concat_axis=0)  100 us
    ppermute x3, waiting for transfers between devices, row_total(): part = part + lax.ppermute(part, 'rows', pairs)  19.7 us
    pallas_call x1, Pallas kernels, jacobi_pallas(): pl.pallas_call(jacobi_kernel, out_shape=jax.ShapeDtypeStruct(gram.shape,...  11.8 us
    pallas_call x1, Pallas kernels, pair_terms(): pl.pallas_call(gram_kernel, out_shape=jax.ShapeDtypeStruct((3, width, wid...  9.1 us
    pallas_call x1, Pallas kernels, rotate_part(): pl.pallas_call(rotate_kernel, out_shape=jax.ShapeDtypeStruct((width, cell...  7.9 us
    ppermute x1, waiting for transfers between devices, partner_2(): return lax.ppermute(value, axis, pairs)  7.29 us
    pallas_call x1, Pallas kernels, lay_out(): pl.pallas_call(lay_kernel, out_shape=[jax.ShapeDtypeStruct((rows_n, local...  6.59 us
    ppermute x3, starting transfers between devices, row_total(): part = part + lax.ppermute(part, 'rows', pairs)  3.83 us
  transfers between devices with their start and end apart: 4, of which 4 were waited for; matrix products, arithmetic and copies ran while one was open for 0% of the time, Pallas kernels for 0%

profile of v1, /device:TPU:0, one launch (start us, length us, event | category | flops | bytes accessed | tf_op | source)
XLA Modules:
  0.0 172.5 jit_solution(6191686981854787954)
XLA Ops:
  0.7 0.0 copy-start.7
  0.7 125.6 %conditional.1 = (f32[128,8192]{1,0:T(8,128)}, f32[128,8192]{1,0:T(8,128)}, f32[3,128,128]{2,1,0:T(8,128)S(1)}) conditional(s32[]{:T(128)} %clamp.3, f32[16,65536]{1,0:T(8,128)} %param.4, f32[16,65536]{1,0:T(8,128)} %param.4), branch_computations={%region_0.0_spmd, %region_1.0_spmd} | conditional | flops 1073889280 | bytes 77791696 | solution.py:268
  0.7 6.6 %branch_0_fun.2 = f32[8,16,8192]{2,1,0:T(8,128)} custom-call(f32[16,65536]{1,0:T(8,128)} %source_ref), custom_call_target="tpu_custom_call" | custom-call | bytes 8388608 | tf_op jit(solution)/shard_map/cond/branch_0_fun/pallas_call | solution.py:173
  7.3 100.5 %all_to_all.20 = f32[8,16,8192]{2,1,0:T(8,128)S(1)} all-to-all(f32[8,16,8192]{2,1,0:T(8,128)} %branch_0_fun.2), channel_id=1, replica_groups=mesh['rows'=8,'cols'=4] {'rows'}, dimensions={0} | all-to-all | bytes 8388608 | tf_op jit(solution)/shard_map/cond/branch_0_fun/all_to_all | solution.py:196
  107.7 2.0 %copy-done = f32[8,16,8192]{2,1,0:T(8,128)} copy-done((f32[8,16,8192]{2,1,0:T(8,128)}, f32[8,16,8192]{2,1,0:T(8,128)S(1)}, u32[]{:S(2)}) %copy-start) | copy-done | bytes 4194328 | tf_op jit(solution)/shard_map/cond
  109.7 0.0 collective-permute-start
  109.7 7.3 %collective-permute-done.theirs_ref = f32[128,8192]{1,0:T(8,128)} collective-permute-done((f32[128,8192]{1,0:T(8,128)S(1)}, f32[128,8192]{1,0:T(8,128)}, u32[]{:S(2)}, u32[]{:S(2)}) %collective-permute-start) | collective-permute-done | bytes 4194336 | tf_op jit(solution)/shard_map/cond/branch_0_fun/ppermute | solution.py:17
  117.0 9.1 %branch_0_fun.3 = f32[3,128,128]{2,1,0:T(8,128)S(1)} custom-call(f32[128,8192]{1,0:T(8,128)} %bitcast.20, f32[128,8192]{1,0:T(8,128)} %collective-permute-done.theirs_ref), custom_call_target="tpu_custom_call" | custom-call | flops 1073741824 | bytes 8388608 | tf_op jit(solution)/shard_map/cond/branch_0_fun/pallas_call | solution.py:136
  126.3 1.5 collective-permute-start.5
  127.8 5.5 %collective-permute-done.5 = f32[3,128,128]{2,1,0:T(8,128)S(1)} collective-permute-done((f32[3,128,128]{2,1,0:T(8,128)S(1)}, f32[3,128,128]{2,1,0:T(8,128)S(1)}, u32[]{:S(2)}, u32[]{:S(2)}) %collective-permute-start.5) | collective-permute-done | bytes 196640 | tf_op jit(solution)/shard_map/ppermute | solution.py:154
  133.3 1.2 collective-permute-start.6
  134.5 5.0 %collective-permute-done.6 = f32[3,128,128]{2,1,0:T(8,128)S(1)} collective-permute-done((f32[3,128,128]{2,1,0:T(8,128)S(1)}, f32[3,128,128]{2,1,0:T(8,128)S(1)}, u32[]{:S(2)}, u32[]{:S(2)}) %collective-permute-start.6) | collective-permute-done | bytes 196640 | tf_op jit(solution)/shard_map/ppermute | solution.py:154
  139.5 1.1 collective-permute-start.7
  140.6 0.0 copy-done.7
  140.7 9.2 %collective-permute-done.7 = f32[3,128,128]{2,1,0:T(8,128)S(1)} collective-permute-done((f32[3,128,128]{2,1,0:T(8,128)S(1)}, f32[3,128,128]{2,1,0:T(8,128)S(1)}, u32[]{:S(2)}, u32[]{:S(2)}) %collective-permute-start.7) | collective-permute-done | bytes 196640 | tf_op jit(solution)/shard_map/ppermute | solution.py:154
  149.9 0.1 copy.11
  150.0 0.1 copy.12
  150.1 0.7 maximum_maximum_fusion.gram_ref
  150.9 11.8 %shard_map.34 = f32[256,256]{1,0:T(8,128)} custom-call(f32[256,256]{1,0:T(8,128)} %maximum_maximum_fusion.gram_ref), custom_call_target="tpu_custom_call" | custom-call | tf_op jit(solution)/shard_map/pallas_call | solution.py:71
  162.6 1.0 fusion
  163.6 0.1 copy.16
  163.7 0.1 copy.15
  163.9 0.7 maximum_bitcast_fusion.coef_ref
  164.6 7.9 %shard_map.35 = f32[128,8192]{1,0:T(8,128)} custom-call(f32[128,256]{1,0:T(8,128)} %maximum_bitcast_fusion.coef_ref, f32[128,8192]{1,0:T(8,128)} %get-tuple-element.35.mine_ref, f32[128,8192]{1,0:T(8,128)} %get-tuple-element.36.theirs_ref), custom_call_target="tpu_custom_call" | custom-call | flops 536870912 | bytes 12582912 | tf_op jit(solution)/shard_map/pallas_call | solution.py:246
  (8 shorter events, 0.1 us)
Async XLA Ops:
  0.7 140.0 %copy-start.7 = (s32[4]{0:T(128)S(1)}, s32[4]{0:T(128)}, u32[]{:S(2)}) copy-start(s32[4]{0:T(128)} %param.5) | copy-start | bytes 52
  107.7 2.0 %copy-start = (f32[8,16,8192]{2,1,0:T(8,128)}, f32[8,16,8192]{2,1,0:T(8,128)S(1)}, u32[]{:S(2)}) copy-start(f32[8,16,8192]{2,1,0:T(8,128)S(1)} %all_to_all.20) | copy-start | bytes 12582916 | tf_op jit(solution)/shard_map/cond
  109.7 7.3 %collective-permute-start = (f32[128,8192]{1,0:T(8,128)S(1)}, f32[128,8192]{1,0:T(8,128)}, u32[]{:S(2)}, u32[]{:S(2)}) collective-permute-start(f32[128,8192]{1,0:T(8,128)S(1)} %bitcast.19), channel_id=1, source_target_pairs={{0,1},{1,0},{2,3},{3,2},{4,5},{5,4},{6,7},{7,6},{8,9},{9,8},{10,11... | collective-permute-start | bytes 12582920 | tf_op jit(solution)/shard_map/cond/branch_0_fun/ppermute | solution.py:17
  126.3 7.0 %collective-permute-start.5 = (f32[3,128,128]{2,1,0:T(8,128)S(1)}, f32[3,128,128]{2,1,0:T(8,128)S(1)}, u32[]{:S(2)}, u32[]{:S(2)}) collective-permute-start(f32[3,128,128]{2,1,0:T(8,128)S(1)} %get-tuple-element.34), channel_id=1, source_target_pairs={{0,4},{4,0},{8,12},{12,8},{16,20},{20,16},{24,28},{28,24},{1,5},{5... | collective-permute-start | bytes 589832 | tf_op jit(solution)/shard_map/ppermute | solution.py:154
  133.3 6.2 %collective-permute-start.6 = (f32[3,128,128]{2,1,0:T(8,128)S(1)}, f32[3,128,128]{2,1,0:T(8,128)S(1)}, u32[]{:S(2)}, u32[]{:S(2)}) collective-permute-start(f32[3,128,128]{2,1,0:T(8,128)S(1)} %add.18), channel_id=1, source_target_pairs={{0,8},{4,12},{8,0},{12,4},{16,24},{20,28},{24,16},{28,20},{1,9},{5... | collective-permute-start | bytes 589832 | tf_op jit(solution)/shard_map/ppermute | solution.py:154
  139.5 10.4 %collective-permute-start.7 = (f32[3,128,128]{2,1,0:T(8,128)S(1)}, f32[3,128,128]{2,1,0:T(8,128)S(1)}, u32[]{:S(2)}, u32[]{:S(2)}) collective-permute-start(f32[3,128,128]{2,1,0:T(8,128)S(1)} %add.19), channel_id=1, source_target_pairs={{0,16},{4,20},{8,24},{12,28},{16,0},{20,4},{24,8},{28,12},{1,17},{... | collective-permute-start | bytes 589832 | tf_op jit(solution)/shard_map/ppermute | solution.py:154

commit v2 on v1

--- a/solution.py
+++ b/solution.py
@@ -218,8 +218,28 @@
     return own_full, other_full, terms
 
 
+def pack_terms(terms):
+    width = terms.shape[1]
+    row = lax.broadcasted_iota(jnp.int32, (width, width), 0)
+    col = lax.broadcasted_iota(jnp.int32, (width, width), 1)
+    shared = jnp.where(row <= col, terms[0], terms[2])
+    diag_theirs = jnp.sum(jnp.where(row == col, terms[2], 0.0), axis=0, keepdims=True)
+    return jnp.concatenate([shared, terms[1], jnp.broadcast_to(diag_theirs, (8, width))], 0)
+
+
+def unpack_terms(packed, width):
+    row = lax.broadcasted_iota(jnp.int32, (width, width), 0)
+    col = lax.broadcasted_iota(jnp.int32, (width, width), 1)
+    shared = packed[:width]
+    gram_mixed = packed[width : 2 * width]
+    diag_theirs = packed[2 * width : 2 * width + 1]
+    gram_mine = jnp.where(row <= col, shared, shared.T)
+    gram_theirs = jnp.where(row > col, shared, jnp.where(row < col, shared.T, diag_theirs))
+    return gram_mine, gram_mixed, gram_theirs
+
+
 def assemble(terms, own_low):
-    gram_mine, gram_mixed, gram_theirs = terms[0], terms[1], terms[2]
+    gram_mine, gram_mixed, gram_theirs = unpack_terms(row_total(pack_terms(terms)), terms.shape[1])
     upper_left = jnp.where(own_low, gram_mine, gram_theirs)
     lower_right = jnp.where(own_low, gram_theirs, gram_mine)
     upper_right = jnp.where(own_low, gram_mixed, gram_mixed.T)
@@ -266,7 +286,7 @@
     own_low = column < partner
     branches = [functools.partial(exchange, bit_pos) for bit_pos in range(bit_count)]
     own_parts, other_parts, terms = lax.switch(bit_index, branches, snapshots)
-    gram_full = assemble(row_total(terms), own_low)
+    gram_full = assemble(terms, own_low)
     rotation = jacobi_pallas(gram_full)
     width = own_parts.shape[0]
     own_columns = jnp.where(own_low, rotation[:, :width], rotation[:, width:])

time: 173 us -> 173 us (level)
  local copies, waits for them, and re-layouts: 3.31 us -> 8.67 us
  waiting for transfers between devices: 27 us -> 21.7 us
    ppermute x3, waiting for transfers between devices: 19.7 us -> 14.4 us  [row_total(): part = part + lax.ppermute(part, 'rows', pairs)]
    cond x2 -> x5, local copies, waits for them, and re-layouts: 1.95 us -> 4.48 us
    slice x0 -> x4, local copies, waits for them, and re-layouts: none -> 1.8 us  [the longest x1 1.61 us: pack_terms(): terms[1]]
where the time goes in v2:
time: 173 us; the launch traced here: 172 us
  blocking collectives  100 us (58%)
  Pallas kernels  36 us (21%)
  waiting for transfers between devices  21.7 us (13%)
  local copies, waits for them, and re-layouts  8.67 us (5%)
  starting transfers between devices  3.83 us (2%)
    all_to_all x1, blocking collectives, spread(): got = lax.all_to_all(sent, 'rows', split_axis=0, concat_axis=0)  100 us
    ppermute x3, waiting for transfers between devices, row_total(): part = part + lax.ppermute(part, 'rows', pairs)  14.4 us
    pallas_call x1, Pallas kernels, jacobi_pallas(): pl.pallas_call(jacobi_kernel, out_shape=jax.ShapeDtypeStruct(gram.shape,...  11.8 us
    pallas_call x1, Pallas kernels, pair_terms(): pl.pallas_call(gram_kernel, out_shape=jax.ShapeDtypeStruct((3, width, wid...  9.78 us
    pallas_call x1, Pallas kernels, rotate_part(): pl.pallas_call(rotate_kernel, out_shape=jax.ShapeDtypeStruct((width, cell...  7.9 us
    ppermute x1, waiting for transfers between devices, partner_2(): return lax.ppermute(value, axis, pairs)  7.29 us
    pallas_call x1, Pallas kernels, lay_out(): pl.pallas_call(lay_kernel, out_shape=[jax.ShapeDtypeStruct((rows_n, local...  6.59 us
    cond x5, local copies, waits for them, and re-layouts  4.48 us
  transfers between devices with their start and end apart: 4, of which 4 were waited for; matrix products, arithmetic and copies ran while one was open for 0% of the time, Pallas kernels for 0%

profile of v2, /device:TPU:0, one launch (start us, length us, event | category | flops | bytes accessed | tf_op | source)
XLA Modules:
  0.0 172.4 jit_solution(16639903603805021122)
XLA Ops:
  0.7 130.2 %conditional.1 = (f32[128,8192]{1,0:T(8,128)}, f32[128,8192]{1,0:T(8,128)}, f32[3,128,128]{2,1,0:T(8,128)}, f32[1,128,128]{2,1,0:T(8,128)}, f32[1,128,128]{2,1,0...) conditional(s32[]{:T(128)} %clamp.3, ...), branch_computations={%region_0.0_spmd, %region_1.0_spmd} | conditional | flops 1073889280 | bytes 78578176 | solution.py:288
  0.7 6.6 %branch_0_fun.2 = f32[8,16,8192]{2,1,0:T(8,128)} custom-call(f32[16,65536]{1,0:T(8,128)} %source_ref), custom_call_target="tpu_custom_call" | custom-call | bytes 8388608 | tf_op jit(solution)/shard_map/cond/branch_0_fun/pallas_call | solution.py:173
  7.3 100.5 %all_to_all.20 = f32[8,16,8192]{2,1,0:T(8,128)S(1)} all-to-all(f32[8,16,8192]{2,1,0:T(8,128)} %branch_0_fun.2), channel_id=1, replica_groups=mesh['rows'=8,'cols'=4] {'rows'}, dimensions={0} | all-to-all | bytes 8388608 | tf_op jit(solution)/shard_map/cond/branch_0_fun/all_to_all | solution.py:196
  107.7 2.0 %copy-done = f32[8,16,8192]{2,1,0:T(8,128)} copy-done((f32[8,16,8192]{2,1,0:T(8,128)}, f32[8,16,8192]{2,1,0:T(8,128)S(1)}, u32[]{:S(2)}) %copy-start) | copy-done | bytes 4194328 | tf_op jit(solution)/shard_map/cond
  109.7 7.3 %collective-permute-done.theirs_ref = f32[128,8192]{1,0:T(8,128)} collective-permute-done((f32[128,8192]{1,0:T(8,128)S(1)}, f32[128,8192]{1,0:T(8,128)}, u32[]{:S(2)}, u32[]{:S(2)}) %collective-permute-start) | collective-permute-done | bytes 4194336 | tf_op jit(solution)/shard_map/cond/branch_0_fun/ppermute | solution.py:17
  117.0 9.8 %branch_0_fun.3 = f32[3,128,128]{2,1,0:T(8,128)} custom-call(f32[128,8192]{1,0:T(8,128)} %bitcast.28, f32[128,8192]{1,0:T(8,128)} %collective-permute-done.theirs_ref), custom_call_target="tpu_custom_call" | custom-call | flops 1073741824 | bytes 8388608 | tf_op jit(solution)/shard_map/cond/branch_0_fun/pallas_call | solution.py:136
  126.8 1.6 fusion.4
  128.4 0.8 copy.55
  129.2 0.8 copy.56
  130.0 0.8 copy.57
  130.9 1.5 collective-permute-start.5
  132.5 4.2 %collective-permute-done.5 = f32[264,128]{1,0:T(8,128)S(1)} collective-permute-done((f32[264,128]{1,0:T(8,128)S(1)}, f32[264,128]{1,0:T(8,128)S(1)}, u32[]{:S(2)}, u32[]{:S(2)}) %collective-permute-start.5) | collective-permute-done | bytes 135200 | tf_op jit(solution)/shard_map/ppermute | solution.py:154
  136.7 1.2 collective-permute-start.6
  137.8 3.9 %collective-permute-done.6 = f32[264,128]{1,0:T(8,128)S(1)} collective-permute-done((f32[264,128]{1,0:T(8,128)S(1)}, f32[264,128]{1,0:T(8,128)S(1)}, u32[]{:S(2)}, u32[]{:S(2)}) %collective-permute-start.6) | collective-permute-done | bytes 135200 | tf_op jit(solution)/shard_map/ppermute | solution.py:154
  141.8 1.1 collective-permute-start.7
  142.9 6.3 %collective-permute-done.7 = f32[264,128]{1,0:T(8,128)S(1)} collective-permute-done((f32[264,128]{1,0:T(8,128)S(1)}, f32[264,128]{1,0:T(8,128)S(1)}, u32[]{:S(2)}, u32[]{:S(2)}) %collective-permute-start.7) | collective-permute-done | bytes 135200 | tf_op jit(solution)/shard_map/ppermute | solution.py:154
  149.6 0.1 copy.15
  150.0 0.8 copy.18.gram_ref
  150.8 11.8 %shard_map.34 = f32[256,256]{1,0:T(8,128)} custom-call(f32[256,256]{1,0:T(8,128)} %copy.18.gram_ref), custom_call_target="tpu_custom_call" | custom-call | tf_op jit(solution)/shard_map/pallas_call | solution.py:71
  162.6 1.0 fusion.6
  163.6 0.1 copy.22
  163.7 0.1 copy.21
  163.8 0.7 maximum_bitcast_fusion.coef_ref
  164.5 7.9 %shard_map.35 = f32[128,8192]{1,0:T(8,128)} custom-call(f32[128,256]{1,0:T(8,128)} %maximum_bitcast_fusion.coef_ref, f32[128,8192]{1,0:T(8,128)} %get-tuple-element.45.mine_ref, f32[128,8192]{1,0:T(8,128)} %get-tuple-element.46.theirs_ref), custom_call_target="tpu_custom_call" | custom-call | flops 536870912 | bytes 12582912 | tf_op jit(solution)/shard_map/pallas_call | solution.py:266
  (22 shorter events, 0.7 us)
Async XLA Ops:
  0.7 142.2 %copy-start.7 = (s32[4]{0:T(128)S(1)}, s32[4]{0:T(128)}, u32[]{:S(2)}) copy-start(s32[4]{0:T(128)} %param.5) | copy-start | bytes 52
  107.7 2.0 %copy-start = (f32[8,16,8192]{2,1,0:T(8,128)}, f32[8,16,8192]{2,1,0:T(8,128)S(1)}, u32[]{:S(2)}) copy-start(f32[8,16,8192]{2,1,0:T(8,128)S(1)} %all_to_all.20) | copy-start | bytes 12582916 | tf_op jit(solution)/shard_map/cond
  109.7 7.3 %collective-permute-start = (f32[128,8192]{1,0:T(8,128)S(1)}, f32[128,8192]{1,0:T(8,128)}, u32[]{:S(2)}, u32[]{:S(2)}) collective-permute-start(f32[128,8192]{1,0:T(8,128)S(1)} %bitcast.27), channel_id=1, source_target_pairs={{0,1},{1,0},{2,3},{3,2},{4,5},{5,4},{6,7},{7,6},{8,9},{9,8},{10,11... | collective-permute-start | bytes 12582920 | tf_op jit(solution)/shard_map/cond/branch_0_fun/ppermute | solution.py:17
  130.9 5.7 %collective-permute-start.5 = (f32[264,128]{1,0:T(8,128)S(1)}, f32[264,128]{1,0:T(8,128)S(1)}, u32[]{:S(2)}, u32[]{:S(2)}) collective-permute-start(f32[264,128]{1,0:T(8,128)S(1)} %pad_maximum_fusion), channel_id=1, source_target_pairs={{0,4},{4,0},{8,12},{12,8},{16,20},{20,16},{24,28},{28,24},{1,5},{5... | collective-permute-start | bytes 405512 | tf_op jit(solution)/shard_map/ppermute | solution.py:154
  136.7 5.1 %collective-permute-start.6 = (f32[264,128]{1,0:T(8,128)S(1)}, f32[264,128]{1,0:T(8,128)S(1)}, u32[]{:S(2)}, u32[]{:S(2)}) collective-permute-start(f32[264,128]{1,0:T(8,128)S(1)} %fusion.2), channel_id=1, source_target_pairs={{0,8},{4,12},{8,0},{12,4},{16,24},{20,28},{24,16},{28,20},{1,9},{5... | collective-permute-start | bytes 405512 | tf_op jit(solution)/shard_map/ppermute | solution.py:154
  141.8 7.5 %collective-permute-start.7 = (f32[264,128]{1,0:T(8,128)S(1)}, f32[264,128]{1,0:T(8,128)S(1)}, u32[]{:S(2)}, u32[]{:S(2)}) collective-permute-start(f32[264,128]{1,0:T(8,128)S(1)} %add.19), channel_id=1, source_target_pairs={{0,16},{4,20},{8,24},{12,28},{16,0},{20,4},{24,8},{28,12},{1,17},{... | collective-permute-start | bytes 405512 | tf_op jit(solution)/shard_map/ppermute | solution.py:154

commit v3 on v2

--- a/solution.py
+++ b/solution.py
@@ -95,9 +95,13 @@
     @pl.when(step == pl.num_programs(0) - 1)
     def _():
         width = mine_ref.shape[0]
-        out_ref[0] = acc_ref[:width, :width]
-        out_ref[1] = acc_ref[:width, width:]
-        out_ref[2] = acc_ref[width:, width:]
+        row = lax.broadcasted_iota(jnp.int32, (width, width), 0)
+        col = lax.broadcasted_iota(jnp.int32, (width, width), 1)
+        gram_theirs = acc_ref[width:, width:]
+        out_ref[:width, :] = jnp.where(row <= col, acc_ref[:width, :width], gram_theirs)
+        out_ref[width : 2 * width, :] = acc_ref[:width, width:]
+        diag_theirs = jnp.sum(jnp.where(row == col, gram_theirs, 0.0), axis=0, keepdims=True)
+        out_ref[2 * width :, :] = jnp.broadcast_to(diag_theirs, (8, width))
 
 
 def gram_store_kernel(mine_ref, theirs_ref, own_in, other_in, out_ref, own_ref, other_ref, acc_ref):
@@ -114,13 +118,13 @@
     return pl.pallas_call(
         gram_store_kernel,
         out_shape=[
-            jax.ShapeDtypeStruct((3, width, width), jnp.float32),
+            jax.ShapeDtypeStruct((2 * width + 8, width), jnp.float32),
             jax.ShapeDtypeStruct(own_full.shape, own_full.dtype),
             jax.ShapeDtypeStruct(other_full.shape, other_full.dtype),
         ],
         grid=(1,),
         in_specs=[cell_spec, cell_spec, pl.BlockSpec(memory_space=pl.ANY), pl.BlockSpec(memory_space=pl.ANY)],
-        out_specs=[pl.BlockSpec((3, width, width), lambda step: (0, 0, 0)), full_spec, full_spec],
+        out_specs=[pl.BlockSpec((2 * width + 8, width), lambda step: (0, 0)), full_spec, full_spec],
         scratch_shapes=[pltpu.VMEM((2 * width, 2 * width), jnp.float32)],
         input_output_aliases={2: 1, 3: 2},
         cost_estimate=pl.CostEstimate(
@@ -135,10 +139,10 @@
     cell_spec = pl.BlockSpec((width, tile), lambda step: (0, step))
     return pl.pallas_call(
         gram_kernel,
-        out_shape=jax.ShapeDtypeStruct((3, width, width), jnp.float32),
+        out_shape=jax.ShapeDtypeStruct((2 * width + 8, width), jnp.float32),
         grid=(cells // tile,),
         in_specs=[cell_spec, cell_spec],
-        out_specs=pl.BlockSpec((3, width, width), lambda step: (0, 0, 0)),
+        out_specs=pl.BlockSpec((2 * width + 8, width), lambda step: (0, 0)),
         scratch_shapes=[pltpu.VMEM((2 * width, 2 * width), jnp.float32)],
         cost_estimate=pl.CostEstimate(
             flops=8 * width * width * cells, transcendentals=0, bytes_accessed=8 * width * cells
@@ -218,15 +222,6 @@
     return own_full, other_full, terms
 
 
-def pack_terms(terms):
-    width = terms.shape[1]
-    row = lax.broadcasted_iota(jnp.int32, (width, width), 0)
-    col = lax.broadcasted_iota(jnp.int32, (width, width), 1)
-    shared = jnp.where(row <= col, terms[0], terms[2])
-    diag_theirs = jnp.sum(jnp.where(row == col, terms[2], 0.0), axis=0, keepdims=True)
-    return jnp.concatenate([shared, terms[1], jnp.broadcast_to(diag_theirs, (8, width))], 0)
-
-
 def unpack_terms(packed, width):
     row = lax.broadcasted_iota(jnp.int32, (width, width), 0)
     col = lax.broadcasted_iota(jnp.int32, (width, width), 1)
@@ -239,7 +234,7 @@
 
 
 def assemble(terms, own_low):
-    gram_mine, gram_mixed, gram_theirs = unpack_terms(row_total(pack_terms(terms)), terms.shape[1])
+    gram_mine, gram_mixed, gram_theirs = unpack_terms(row_total(terms), terms.shape[1])
     upper_left = jnp.where(own_low, gram_mine, gram_theirs)
     lower_right = jnp.where(own_low, gram_theirs, gram_mine)
     upper_right = jnp.where(own_low, gram_mixed, gram_mixed.T)

time: 173 us -> 168 us (0.971)
  local copies, waits for them, and re-layouts: 8.67 us -> 4.54 us
    cond x5 -> x2, local copies, waits for them, and re-layouts: 4.48 us -> 1.97 us
where the time goes in v3:
time: 168 us
  blocking collectives  100 us (60%)
  Pallas kernels  35.4 us (21%)
  waiting for transfers between devices  21.7 us (13%)
  local copies, waits for them, and re-layouts  4.54 us (3%)
  starting transfers between devices  3.83 us (2%)
    all_to_all x1, blocking collectives, spread(): got = lax.all_to_all(sent, 'rows', split_axis=0, concat_axis=0)  100 us
    ppermute x3, waiting for transfers between devices, row_total(): part = part + lax.ppermute(part, 'rows', pairs)  14.4 us
    pallas_call x1, Pallas kernels, jacobi_pallas(): pl.pallas_call(jacobi_kernel, out_shape=jax.ShapeDtypeStruct(gram.shape,...  11.8 us
    pallas_call x1, Pallas kernels, pair_terms(): pl.pallas_call(gram_kernel, out_shape=jax.ShapeDtypeStruct((2 * width + 8...  9.11 us
    pallas_call x1, Pallas kernels, rotate_part(): pl.pallas_call(rotate_kernel, out_shape=jax.ShapeDtypeStruct((width, cell...  7.9 us
    ppermute x1, waiting for transfers between devices, partner_2(): return lax.ppermute(value, axis, pairs)  7.29 us
    pallas_call x1, Pallas kernels, lay_out(): pl.pallas_call(lay_kernel, out_shape=[jax.ShapeDtypeStruct((rows_n, local...  6.59 us
    ppermute x3, starting transfers between devices, row_total(): part = part + lax.ppermute(part, 'rows', pairs)  3.82 us
  transfers between devices with their start and end apart: 4, of which 4 were waited for; matrix products, arithmetic and copies ran while one was open for 0% of the time, Pallas kernels for 0%

profile of v3, /device:TPU:0, one launch (start us, length us, event | category | flops | bytes accessed | tf_op | source)
XLA Modules:
  0.0 167.8 jit_solution(8544157301407728045)
XLA Ops:
  0.7 125.6 %conditional.1 = (f32[128,8192]{1,0:T(8,128)}, f32[128,8192]{1,0:T(8,128)}, f32[264,128]{1,0:T(8,128)S(1)}) conditional(s32[]{:T(128)} %clamp.3, f32[16,65536]{1,0:T(8,128)} %param.4, f32[16,65536]{1,0:T(8,128)} %param.4), branch_computations={%region_0.0_spmd, %region_1.0_spmd} | conditional | flops 1073843200 | bytes 76747216 | solution.py:283
  0.7 6.6 %branch_0_fun.2 = f32[8,16,8192]{2,1,0:T(8,128)} custom-call(f32[16,65536]{1,0:T(8,128)} %source_ref), custom_call_target="tpu_custom_call" | custom-call | bytes 8388608 | tf_op jit(solution)/shard_map/cond/branch_0_fun/pallas_call | solution.py:177
  7.3 100.5 %all_to_all.20 = f32[8,16,8192]{2,1,0:T(8,128)S(1)} all-to-all(f32[8,16,8192]{2,1,0:T(8,128)} %branch_0_fun.2), channel_id=1, replica_groups=mesh['rows'=8,'cols'=4] {'rows'}, dimensions={0} | all-to-all | bytes 8388608 | tf_op jit(solution)/shard_map/cond/branch_0_fun/all_to_all | solution.py:200
  107.7 2.0 %copy-done = f32[8,16,8192]{2,1,0:T(8,128)} copy-done((f32[8,16,8192]{2,1,0:T(8,128)}, f32[8,16,8192]{2,1,0:T(8,128)S(1)}, u32[]{:S(2)}) %copy-start) | copy-done | bytes 4194328 | tf_op jit(solution)/shard_map/cond
  109.7 7.3 %collective-permute-done.theirs_ref = f32[128,8192]{1,0:T(8,128)} collective-permute-done((f32[128,8192]{1,0:T(8,128)S(1)}, f32[128,8192]{1,0:T(8,128)}, u32[]{:S(2)}, u32[]{:S(2)}) %collective-permute-start) | collective-permute-done | bytes 4194336 | tf_op jit(solution)/shard_map/cond/branch_0_fun/ppermute | solution.py:17
  117.0 9.1 %branch_0_fun.3 = f32[264,128]{1,0:T(8,128)S(1)} custom-call(f32[128,8192]{1,0:T(8,128)} %bitcast.22, f32[128,8192]{1,0:T(8,128)} %collective-permute-done.theirs_ref), custom_call_target="tpu_custom_call" | custom-call | flops 1073741824 | bytes 8388608 | tf_op jit(solution)/shard_map/cond/branch_0_fun/pallas_call | solution.py:140
  126.3 1.5 collective-permute-start.5
  127.8 4.2 %collective-permute-done.5 = f32[264,128]{1,0:T(8,128)S(1)} collective-permute-done((f32[264,128]{1,0:T(8,128)S(1)}, f32[264,128]{1,0:T(8,128)S(1)}, u32[]{:S(2)}, u32[]{:S(2)}) %collective-permute-start.5) | collective-permute-done | bytes 135200 | tf_op jit(solution)/shard_map/ppermute | solution.py:158
  132.0 1.2 collective-permute-start.6
  133.2 3.9 %collective-permute-done.6 = f32[264,128]{1,0:T(8,128)S(1)} collective-permute-done((f32[264,128]{1,0:T(8,128)S(1)}, f32[264,128]{1,0:T(8,128)S(1)}, u32[]{:S(2)}, u32[]{:S(2)}) %collective-permute-start.6) | collective-permute-done | bytes 135200 | tf_op jit(solution)/shard_map/ppermute | solution.py:158
  137.1 1.1 collective-permute-start.7
  138.3 6.3 %collective-permute-done.7 = f32[264,128]{1,0:T(8,128)S(1)} collective-permute-done((f32[264,128]{1,0:T(8,128)S(1)}, f32[264,128]{1,0:T(8,128)S(1)}, u32[]{:S(2)}, u32[]{:S(2)}) %collective-permute-start.7) | collective-permute-done | bytes 135200 | tf_op jit(solution)/shard_map/ppermute | solution.py:158
  144.7 0.1 copy.11
  144.9 0.1 copy.16
  145.0 0.1 copy.15
  145.1 0.1 copy.13
  145.2 0.1 copy.17
  145.3 0.8 copy.18.gram_ref
  146.2 11.8 %shard_map.34 = f32[256,256]{1,0:T(8,128)} custom-call(f32[256,256]{1,0:T(8,128)} %copy.18.gram_ref), custom_call_target="tpu_custom_call" | custom-call | tf_op jit(solution)/shard_map/pallas_call | solution.py:71
  158.0 1.0 fusion.2
  158.9 0.1 copy.22
  159.0 0.1 copy.21
  159.2 0.7 maximum_bitcast_fusion.coef_ref
  159.9 7.9 %shard_map.35 = f32[128,8192]{1,0:T(8,128)} custom-call(f32[128,256]{1,0:T(8,128)} %maximum_bitcast_fusion.coef_ref, f32[128,8192]{1,0:T(8,128)} %get-tuple-element.35.mine_ref, f32[128,8192]{1,0:T(8,128)} %get-tuple-element.36.theirs_ref), custom_call_target="tpu_custom_call" | custom-call | flops 536870912 | bytes 12582912 | tf_op jit(solution)/shard_map/pallas_call | solution.py:261
  (15 shorter events, 0.3 us)
Async XLA Ops:
  0.7 137.6 %copy-start.7 = (s32[4]{0:T(128)S(1)}, s32[4]{0:T(128)}, u32[]{:S(2)}) copy-start(s32[4]{0:T(128)} %param.5) | copy-start | bytes 52
  107.7 2.0 %copy-start = (f32[8,16,8192]{2,1,0:T(8,128)}, f32[8,16,8192]{2,1,0:T(8,128)S(1)}, u32[]{:S(2)}) copy-start(f32[8,16,8192]{2,1,0:T(8,128)S(1)} %all_to_all.20) | copy-start | bytes 12582916 | tf_op jit(solution)/shard_map/cond
  109.7 7.3 %collective-permute-start = (f32[128,8192]{1,0:T(8,128)S(1)}, f32[128,8192]{1,0:T(8,128)}, u32[]{:S(2)}, u32[]{:S(2)}) collective-permute-start(f32[128,8192]{1,0:T(8,128)S(1)} %bitcast.21), channel_id=1, source_target_pairs={{0,1},{1,0},{2,3},{3,2},{4,5},{5,4},{6,7},{7,6},{8,9},{9,8},{10,11... | collective-permute-start | bytes 12582920 | tf_op jit(solution)/shard_map/cond/branch_0_fun/ppermute | solution.py:17
  126.3 5.7 %collective-permute-start.5 = (f32[264,128]{1,0:T(8,128)S(1)}, f32[264,128]{1,0:T(8,128)S(1)}, u32[]{:S(2)}, u32[]{:S(2)}) collective-permute-start(f32[264,128]{1,0:T(8,128)S(1)} %get-tuple-element.34), channel_id=1, source_target_pairs={{0,4},{4,0},{8,12},{12,8},{16,20},{20,16},{24,28},{28,24},{1,5},{5... | collective-permute-start | bytes 405512 | tf_op jit(solution)/shard_map/ppermute | solution.py:158
  132.0 5.1 %collective-permute-start.6 = (f32[264,128]{1,0:T(8,128)S(1)}, f32[264,128]{1,0:T(8,128)S(1)}, u32[]{:S(2)}, u32[]{:S(2)}) collective-permute-start(f32[264,128]{1,0:T(8,128)S(1)} %add.18), channel_id=1, source_target_pairs={{0,8},{4,12},{8,0},{12,4},{16,24},{20,28},{24,16},{28,20},{1,9},{5... | collective-permute-start | bytes 405512 | tf_op jit(solution)/shard_map/ppermute | solution.py:158
  137.1 7.5 %collective-permute-start.7 = (f32[264,128]{1,0:T(8,128)S(1)}, f32[264,128]{1,0:T(8,128)S(1)}, u32[]{:S(2)}, u32[]{:S(2)}) collective-permute-start(f32[264,128]{1,0:T(8,128)S(1)} %add.19), channel_id=1, source_target_pairs={{0,16},{4,20},{8,24},{12,28},{16,0},{20,4},{24,8},{28,12},{1,17},{... | collective-permute-start | bytes 405512 | tf_op jit(solution)/shard_map/ppermute | solution.py:158

commit v4 on v3

--- a/solution.py
+++ b/solution.py
@@ -163,24 +163,25 @@
 CHUNKS = 4
 
 
-def lay_kernel(source_ref, *out_refs):
-    piece = out_refs[0].shape[-1]
-    for chunk, out_ref in enumerate(out_refs):
+def lay_kernel(chunk_ids, piece, source_ref, *out_refs):
+    for chunk, out_ref in zip(chunk_ids, out_refs):
         out_ref[...] = source_ref[:, chunk * piece : (chunk + 1) * piece]
 
 
-def lay_out(snapshots, rows_n, chunks):
+def lay_out(snapshots, rows_n, chunks, chunk_ids):
     local_rows, cells = snapshots.shape
     width = cells // rows_n
     piece = width // chunks
     out_spec = pl.BlockSpec((None, local_rows, piece), lambda dest: (dest, 0, 0))
     return pl.pallas_call(
-        lay_kernel,
-        out_shape=[jax.ShapeDtypeStruct((rows_n, local_rows, piece), snapshots.dtype)] * chunks,
+        functools.partial(lay_kernel, tuple(chunk_ids), piece),
+        out_shape=[jax.ShapeDtypeStruct((rows_n, local_rows, piece), snapshots.dtype)] * len(chunk_ids),
         grid=(rows_n,),
         in_specs=[pl.BlockSpec((local_rows, width), lambda dest: (0, dest))],
-        out_specs=[out_spec] * chunks,
-        cost_estimate=pl.CostEstimate(flops=0, transcendentals=0, bytes_accessed=8 * local_rows * cells),
+        out_specs=[out_spec] * len(chunk_ids),
+        cost_estimate=pl.CostEstimate(
+            flops=0, transcendentals=0, bytes_accessed=8 * local_rows * piece * rows_n * len(chunk_ids)
+        ),
     )(snapshots)
 
 
@@ -191,7 +192,12 @@
     width = cells // rows_n
     piece = width // chunks
 
-    sends = lay_out(snapshots, rows_n, chunks)
+    if chunks == 1:
+        mine = lax.all_to_all(snapshots, "rows", split_axis=1, concat_axis=0, tiled=True)
+        theirs = partner_2(mine, "cols", bit_pos)
+        return mine, theirs, pair_terms(mine, theirs)
+
+    sends = lay_out(snapshots, rows_n, chunks, [0]) + lay_out(snapshots, rows_n, chunks, range(1, chunks))
 
     def laid(chunk):
         return sends[chunk]
@@ -211,8 +217,6 @@
         other_parts.append(partner_2(held[0], "cols", bit_pos))
         own_parts.append(spread(held[1]))
     other_parts.append(partner_2(own_parts[-1], "cols", bit_pos))
-    if chunks == 1:
-        return own_parts[0], other_parts[0], pair_terms(own_parts[0], other_parts[0])
     own_full = jnp.zeros((rows_n * local_rows, width), snapshots.dtype)
     other_full = jnp.zeros((rows_n * local_rows, width), snapshots.dtype)
     terms = None

time: 168 us -> 164 us (0.976)
  Pallas kernels: 35.4 us -> 28.8 us
  local copies, waits for them, and re-layouts: 4.54 us -> 7.02 us
    pallas_call x1 -> x0, Pallas kernels: 6.59 us -> none  [lay_out(): pl.pallas_call(lay_kernel, out_shape=[jax.ShapeDtypeStruct((rows_n, local...]
    all_to_all x0 -> x1, local copies, waits for them, and re-layouts: none -> 2.49 us  [exchange(): lax.all_to_all(snapshots, 'rows', split_axis=1, concat_axis=0, tiled=True)]
where the time goes in v4:
time: 164 us; the launch traced here: 163 us
  blocking collectives  100 us (61%)
  Pallas kernels  28.8 us (18%)
  waiting for transfers between devices  21.7 us (13%)
  local copies, waits for them, and re-layouts  7.02 us (4%)
  starting transfers between devices  3.83 us (2%)
    all_to_all x1, blocking collectives, exchange(): lax.all_to_all(snapshots, 'rows', split_axis=1, concat_axis=0, tiled=True)  100 us
    ppermute x3, waiting for transfers between devices, row_total(): part = part + lax.ppermute(part, 'rows', pairs)  14.4 us
    pallas_call x1, Pallas kernels, jacobi_pallas(): pl.pallas_call(jacobi_kernel, out_shape=jax.ShapeDtypeStruct(gram.shape,...  11.8 us
    pallas_call x1, Pallas kernels, pair_terms(): pl.pallas_call(gram_kernel, out_shape=jax.ShapeDtypeStruct((2 * width + 8...  9.12 us
    pallas_call x1, Pallas kernels, rotate_part(): pl.pallas_call(rotate_kernel, out_shape=jax.ShapeDtypeStruct((width, cell...  7.9 us
    ppermute x1, waiting for transfers between devices, partner_2(): return lax.ppermute(value, axis, pairs)  7.29 us
    ppermute x3, starting transfers between devices, row_total(): part = part + lax.ppermute(part, 'rows', pairs)  3.82 us
  transfers between devices with their start and end apart: 4, of which 4 were waited for; matrix products, arithmetic and copies ran while one was open for 0% of the time, Pallas kernels for 0%

profile of v4, /device:TPU:0, one launch (start us, length us, event | category | flops | bytes accessed | tf_op | source)
XLA Modules:
  0.0 163.4 jit_solution(2950864908267454935)
XLA Ops:
  0.7 121.3 %conditional.1 = (f32[128,8192]{1,0:T(8,128)}, f32[128,8192]{1,0:T(8,128)}, f32[264,128]{1,0:T(8,128)S(1)}) conditional(s32[]{:T(128)} %clamp.3, f32[16,65536]{1,0:T(8,128)} %param.4, f32[16,65536]{1,0:T(8,128)} %param.4), branch_computations={%region_0.0_spmd, %region_1.0_spmd} | conditional | flops 1073843200 | bytes 77795824 | solution.py:287
  0.7 2.5 %copy.26 = f32[2,8,8,8192]{3,2,0,1:T(8,128)S(1)} copy(f32[2,8,8,8192]{3,2,1,0:T(8,128)} %bitcast.30) | data formatting | bytes 8388608 | tf_op jit(solution)/shard_map/cond/branch_0_fun/all_to_all | solution.py:196
  3.2 100.3 %all_to_all.31 = f32[16,8,8192]{2,0,1:T(8,128)S(1)} all-to-all(f32[16,8,8192]{2,0,1:T(8,128)S(1)} %bitcast.31), channel_id=1, replica_groups=mesh['rows'=8,'cols'=4] {'rows'}, dimensions={1} | all-to-all | bytes 8388608 | tf_op jit(solution)/shard_map/cond/branch_0_fun/all_to_all | solution.py:196
  103.4 2.0 %copy-done = f32[16,8,8192]{2,0,1:T(8,128)} copy-done((f32[16,8,8192]{2,0,1:T(8,128)}, f32[16,8,8192]{2,0,1:T(8,128)S(1)}, u32[]{:S(2)}) %copy-start) | copy-done | bytes 4194328 | tf_op jit(solution)/shard_map/cond
  105.4 7.3 %collective-permute-done.theirs_ref = f32[128,8192]{1,0:T(8,128)} collective-permute-done((f32[128,8192]{1,0:T(8,128)S(1)}, f32[128,8192]{1,0:T(8,128)}, u32[]{:S(2)}, u32[]{:S(2)}) %collective-permute-start) | collective-permute-done | bytes 4194336 | tf_op jit(solution)/shard_map/cond/branch_0_fun/ppermute | solution.py:17
  112.7 9.1 %branch_0_fun.1 = f32[264,128]{1,0:T(8,128)S(1)} custom-call(f32[128,8192]{1,0:T(8,128)} %bitcast.28, f32[128,8192]{1,0:T(8,128)} %collective-permute-done.theirs_ref), custom_call_target="tpu_custom_call" | custom-call | flops 1073741824 | bytes 8388608 | tf_op jit(solution)/shard_map/cond/branch_0_fun/pallas_call | solution.py:140
  122.0 1.5 collective-permute-start.5
  123.5 4.2 %collective-permute-done.5 = f32[264,128]{1,0:T(8,128)S(1)} collective-permute-done((f32[264,128]{1,0:T(8,128)S(1)}, f32[264,128]{1,0:T(8,128)S(1)}, u32[]{:S(2)}, u32[]{:S(2)}) %collective-permute-start.5) | collective-permute-done | bytes 135200 | tf_op jit(solution)/shard_map/ppermute | solution.py:158
  127.7 1.2 collective-permute-start.6
  128.9 3.9 %collective-permute-done.6 = f32[264,128]{1,0:T(8,128)S(1)} collective-permute-done((f32[264,128]{1,0:T(8,128)S(1)}, f32[264,128]{1,0:T(8,128)S(1)}, u32[]{:S(2)}, u32[]{:S(2)}) %collective-permute-start.6) | collective-permute-done | bytes 135200 | tf_op jit(solution)/shard_map/ppermute | solution.py:158
  132.8 1.1 collective-permute-start.7
  134.0 6.3 %collective-permute-done.7 = f32[264,128]{1,0:T(8,128)S(1)} collective-permute-done((f32[264,128]{1,0:T(8,128)S(1)}, f32[264,128]{1,0:T(8,128)S(1)}, u32[]{:S(2)}, u32[]{:S(2)}) %collective-permute-start.7) | collective-permute-done | bytes 135200 | tf_op jit(solution)/shard_map/ppermute | solution.py:158
  140.5 0.1 copy.14
  140.6 0.1 copy.16
  140.7 0.1 copy.17
  140.8 0.1 copy.18
  140.9 0.1 copy.15
  141.0 0.8 copy.19.gram_ref
  141.9 11.8 %shard_map.34 = f32[256,256]{1,0:T(8,128)} custom-call(f32[256,256]{1,0:T(8,128)} %copy.19.gram_ref), custom_call_target="tpu_custom_call" | custom-call | tf_op jit(solution)/shard_map/pallas_call | solution.py:71
  153.7 1.0 fusion.2
  154.6 0.1 copy.22
  154.7 0.1 copy.23
  154.9 0.7 maximum_bitcast_fusion.coef_ref
  155.5 7.9 %shard_map.35 = f32[128,8192]{1,0:T(8,128)} custom-call(f32[128,256]{1,0:T(8,128)} %maximum_bitcast_fusion.coef_ref, f32[128,8192]{1,0:T(8,128)} %get-tuple-element.34.mine_ref, f32[128,8192]{1,0:T(8,128)} %get-tuple-element.35.theirs_ref), custom_call_target="tpu_custom_call" | custom-call | flops 536870912 | bytes 12582912 | tf_op jit(solution)/shard_map/pallas_call | solution.py:265
  (15 shorter events, 0.3 us)
Async XLA Ops:
  0.7 133.3 %copy-start.7 = (s32[4]{0:T(128)S(1)}, s32[4]{0:T(128)}, u32[]{:S(2)}) copy-start(s32[4]{0:T(128)} %param.5) | copy-start | bytes 52
  103.4 2.0 %copy-start = (f32[16,8,8192]{2,0,1:T(8,128)}, f32[16,8,8192]{2,0,1:T(8,128)S(1)}, u32[]{:S(2)}) copy-start(f32[16,8,8192]{2,0,1:T(8,128)S(1)} %all_to_all.31) | copy-start | bytes 12582916 | tf_op jit(solution)/shard_map/cond
  105.4 7.3 %collective-permute-start = (f32[128,8192]{1,0:T(8,128)S(1)}, f32[128,8192]{1,0:T(8,128)}, u32[]{:S(2)}, u32[]{:S(2)}) collective-permute-start(f32[128,8192]{1,0:T(8,128)S(1)} %bitcast.27), channel_id=1, source_target_pairs={{0,1},{1,0},{2,3},{3,2},{4,5},{5,4},{6,7},{7,6},{8,9},{9,8},{10,11... | collective-permute-start | bytes 12582920 | tf_op jit(solution)/shard_map/cond/branch_0_fun/ppermute | solution.py:17
  122.0 5.7 %collective-permute-start.5 = (f32[264,128]{1,0:T(8,128)S(1)}, f32[264,128]{1,0:T(8,128)S(1)}, u32[]{:S(2)}, u32[]{:S(2)}) collective-permute-start(f32[264,128]{1,0:T(8,128)S(1)} %get-tuple-element.33), channel_id=1, source_target_pairs={{0,4},{4,0},{8,12},{12,8},{16,20},{20,16},{24,28},{28,24},{1,5},{5... | collective-permute-start | bytes 405512 | tf_op jit(solution)/shard_map/ppermute | solution.py:158
  127.7 5.1 %collective-permute-start.6 = (f32[264,128]{1,0:T(8,128)S(1)}, f32[264,128]{1,0:T(8,128)S(1)}, u32[]{:S(2)}, u32[]{:S(2)}) collective-permute-start(f32[264,128]{1,0:T(8,128)S(1)} %add.18), channel_id=1, source_target_pairs={{0,8},{4,12},{8,0},{12,4},{16,24},{20,28},{24,16},{28,20},{1,9},{5... | collective-permute-start | bytes 405512 | tf_op jit(solution)/shard_map/ppermute | solution.py:158
  132.8 7.5 %collective-permute-start.7 = (f32[264,128]{1,0:T(8,128)S(1)}, f32[264,128]{1,0:T(8,128)S(1)}, u32[]{:S(2)}, u32[]{:S(2)}) collective-permute-start(f32[264,128]{1,0:T(8,128)S(1)} %add.19), channel_id=1, source_target_pairs={{0,16},{4,20},{8,24},{12,28},{16,0},{20,4},{24,8},{28,12},{1,17},{... | collective-permute-start | bytes 405512 | tf_op jit(solution)/shard_map/ppermute | solution.py:158
